TPU v7x, 256 devices: a whole 4x4x8 slice. The times are simulated.
256 devices in a mesh: replica: 16 (over y_lo, x, core), fsdp: 16 (over z, y_hi).
Axes of the slice: x: 4, y: 4 (y_hi: 2, y_lo: 2; y = y_hi * 2 + y_lo), z: 8, core: 2. Of those that a mesh axis runs over, the one named last changes fastest.
Arguments:
- activations: bfloat16 [65536, 8192], P(('replica', 'fsdp')), may hold values from -6 to 6
- cotangent: bfloat16 [65536, 512], P(('replica', 'fsdp')), may hold values from -12288 to 12288
- labels: int32 [65536], P(('replica', 'fsdp')), may hold values from -1 to 128255, as said below
- local_weight: float32 [16, 8192, 512], P('replica', 'fsdp'), may hold values from -4.5 to 4.5
- first_moment: bfloat16 [16, 8192, 512], P('replica', 'fsdp'), may hold values from -1.75 to 1.75
- second_moment: bfloat16 [16, 8192, 512], P('replica', 'fsdp'), may hold values from 0.019897461 to 2
- anchor_weight: float32 [8192, 512], P('fsdp'), may hold values from -4 to 4
- outer_state: float32 [8192, 512], P('fsdp'), may hold values from -1.75 to 1.75
Outputs:
- input_grad: bfloat16 [65536, 8192], P(('replica', 'fsdp'))
- new_anchor: float32 [8192, 512], P('fsdp')
- new_state: float32 [8192, 512], P('fsdp')
- new_first: bfloat16 [16, 8192, 512], P('replica', 'fsdp')
- new_second: bfloat16 [16, 8192, 512], P('replica', 'fsdp')
Inputs may be any that keep to these rules, and one draw needn't show every extreme that they name: `labels`: each worker's tokens begin with a prompt of at least 512 tokens, labelled -1, and all later tokens carry ids of 0 to 128255; at least 512 of them do.
All inputs are finite; a program needn't handle non-finite values.
Results may differ from a plain program's by a relative error of at most 0.0059.
Values may be sent and summed in bfloat16 or wider, within the bound.
No kernel may reach another device: no remote copies, remote signals or barrier semaphores. Data moves between devices by JAX's collectives and lax.ppermute only.
A program may use at most 128 MiB of HBM per device.

v0:
```python
import jax
import jax.numpy as jnp
from jax import lax
from jax.sharding import PartitionSpec as P

D = 8192
norm_eps = 1e-05
beta_first = 0.9
beta_second = 0.95
adam_eps = 1e-08
weight_decay = 0.1
inner_rate = 0.1
outer_rate = 0.7
outer_momentum = 0.9


def contract_last(left, right):
    return lax.dot_general(
        left, right, (((1,), (1,)), ((), ())), preferred_element_type=jnp.float32
    )


def contract_first(left, right):
    return lax.dot_general(
        left, right, (((0,), (0,)), ((), ())), preferred_element_type=jnp.float32
    )


def per_device(
    activations,
    cotangent,
    labels,
    local_weight,
    first_moment,
    second_moment,
    anchor_weight,
    outer_state,
):
    width_scale = D ** (-0.5)
    weight_shard = local_weight[0]
    weight_low = weight_shard.astype(jnp.bfloat16)
    answer = (labels >= 0).astype(jnp.float32)
    values = activations.astype(jnp.float32)
    inverse = lax.rsqrt(jnp.mean(values * values, axis=1, keepdims=True) + norm_eps)
    normed = values * inverse
    normed_low = normed.astype(jnp.bfloat16)
    answers = lax.psum(jnp.sum(answer), "fsdp")
    scaled = (cotangent.astype(jnp.float32) * answer[:, None] / answers).astype(jnp.bfloat16)
    feature_grad = width_scale * contract_last(
        scaled, lax.all_gather(weight_low, "fsdp", axis=0, tiled=True)
    )
    projected = jnp.mean(feature_grad * normed, axis=1, keepdims=True)
    input_grad = (inverse * (feature_grad - normed * projected)).astype(jnp.bfloat16)
    gradient = lax.psum_scatter(
        (width_scale * contract_first(normed_low, scaled)).astype(jnp.bfloat16),
        "fsdp",
        scatter_dimension=0,
        tiled=True,
    ).astype(jnp.float32)
    first = beta_first * first_moment[0].astype(jnp.float32) + (1.0 - beta_first) * gradient
    second = (
        beta_second * second_moment[0].astype(jnp.float32)
        + (1.0 - beta_second) * gradient * gradient
    )
    stepped = weight_shard - inner_rate * (
        first / (jnp.sqrt(second) + adam_eps) + weight_decay * weight_shard
    )
    pseudo_grad = anchor_weight - stepped
    replicas = lax.axis_size("replica")
    average = lax.psum(pseudo_grad.astype(jnp.bfloat16), "replica").astype(jnp.float32) / replicas
    new_state = outer_momentum * outer_state + average
    new_anchor = anchor_weight - outer_rate * (average + outer_momentum * new_state)
    new_first = first.astype(jnp.bfloat16)[None]
    new_second = second.astype(jnp.bfloat16)[None]
    return (input_grad, new_anchor, new_state, new_first, new_second)


def solution(mesh):
    in_specs = (
        P(("replica", "fsdp"), None),
        P(("replica", "fsdp"), None),
        P(("replica", "fsdp")),
        P("replica", "fsdp", None),
        P("replica", "fsdp", None),
        P("replica", "fsdp", None),
        P("fsdp", None),
        P("fsdp", None),
    )
    out_specs = (
        P(("replica", "fsdp"), None),
        P("fsdp", None),
        P("fsdp", None),
        P("replica", "fsdp", None),
        P("replica", "fsdp", None),
    )
    return jax.shard_map(
        per_device, mesh=mesh, in_specs=in_specs, out_specs=out_specs, check_vma=False
    )
```

profile of v0, /device:TPU:1, one launch (start us, length us, event | category | flops | bytes accessed | tf_op | source)
XLA Modules:
  0.0 511.3 jit_solution(3030680337738197865)
XLA Ops:
  7.2 0.0 all-gather.2.cloned.1.call-start
  7.2 2.1 bitcast_convert_fusion
  9.3 0.0 all-gather.2.cloned.1.call-update
  9.3 0.0 reduce-scatter.2.cloned.1.call-start
  9.4 1.3 fusion.20
  10.7 39.4 %psum.14 = f32[]{:T(128)} all-reduce(f32[]{:T(128)} %fusion.20), channel_id=1, replica_groups=mesh['replica'=16,'fsdp'=16] {'fsdp'}, use_global_device_ids=true, to_apply=%region_2.0 | all-reduce | flops 1 | bytes 8 | tf_op jit(solution)/shard_map/psum | solution.py:47
  50.1 0.7 compare_convert_fusion
  50.8 3.1 fusion.7
  53.9 8.6 %multiply_convert_fusion = bf16[8192,512]{1,0:T(8,128)(2,1)} fusion(bf16[256,8192]{1,0:T(8,128)(2,1)} %param.8, f32[256]{0:T(256)S(1)} %add_rsqrt_fusion, bf16[256,512]{1,0:T(8,128)(2,1)} %param.9, f32[]{:T(128)} %psum.14, f32[256]{0:T(256)S(1)} %compare_convert_fusion), kind=kOutput, calls=%fused_computation | convolution fusion | flops 2162688000 | bytes 12847108 | tf_op jit(solution)/shard_map/dot_general | solution.py:24
  62.5 0.0 copy-start.5
  62.5 0.0 reduce-scatter.2.cloned.1.call-update
  62.5 0.0 copy-start
  62.6 0.0 copy-start.1
  62.6 0.0 copy-start.3
  62.6 0.0 copy-start.4
  62.6 0.0 all-reduce.2.cloned.1.call-start
  62.6 87.0 %all-gather.2.cloned.1.call-done = bf16[8192,512]{1,0:T(8,128)(2,1)} async-done(((bf16[512,512]{1,0:T(8,128)(2,1)}), bf16[8192,512]{1,0:T(8,128)(2,1)}) %all-gather.2.cloned.1.call-update) | async-done | bytes 8388624 | tf_op jit(solution)/shard_map/all_gather | solution.py:50
  149.6 0.0 copy-done.5
  149.6 12.5 %fusion.3 = (f32[256]{0:T(256)S(1)}, f32[256,8192]{1,0:T(8,128)}) fusion(bf16[256,8192]{1,0:T(8,128)(2,1)} %param.8, f32[256]{0:T(256)S(1)} %add_rsqrt_fusion, bf16[8192,512]{1,0:T(8,128)(2,1)} %all-gather.2.cloned.1.call-done, bf16[256,512]{1,0:T(8,128)(2,1)S(1)} %copy-done.5, f32[]{:T(128)} %psum.14, f32[256]{0:T(256)S(1)} %compare_convert_fusion), kind=kOutput, calls=%fused_computation.7 | convolution fusion | flops 2158493440 | bytes 21236740 | tf_op jit(solution)/shard_map/dot_general | solution.py:18
  162.2 210.8 %reduce-scatter.2.cloned.1.call-done = bf16[512,512]{1,0:T(8,128)(2,1)} async-done(((bf16[8192,512]{1,0:T(8,128)(2,1)}), bf16[512,512]{1,0:T(8,128)(2,1)}) %reduce-scatter.2.cloned.1.call-update) | async-done | bytes 524304 | tf_op jit(solution)/shard_map/reduce_scatter | solution.py:54
  373.0 0.0 copy-done
  373.0 0.0 copy-done.1
  373.0 0.0 copy-done.3
  373.0 0.0 copy-done.4
  373.0 3.2 fusion.18
  376.1 0.0 all-reduce.2.cloned.1.call-update
  376.2 0.0 copy-start.2
  376.2 6.9 %fusion.6 = bf16[256,8192]{1,0:T(8,128)(2,1)} fusion(f32[256,8192]{1,0:T(8,128)} %get-tuple-element.11, bf16[256,8192]{1,0:T(8,128)(2,1)} %param.8, f32[256]{0:T(256)S(1)} %broadcast_multiply_fusion, f32[256]{0:T(256)S(1)} %add_rsqrt_fusion), kind=kLoop, calls=%fused_computation.10 | loop fusion | flops 12582912 | bytes 16779264 | tf_op jit(solution)/shard_map/convert_element_type | solution.py:53
  383.1 119.0 %all-reduce.2.cloned.1.call-done = bf16[512,512]{1,0:T(8,128)(2,1)} async-done(((bf16[512,512]{1,0:T(8,128)(2,1)}), bf16[512,512]{1,0:T(8,128)(2,1)}) %all-reduce.2.cloned.1.call-update) | async-done | bytes 524304 | tf_op jit(solution)/shard_map/psum | solution.py:70
  502.1 0.0 copy-done.2
  502.1 2.7 multiply_subtract_fusion
  (2 shorter events, 0.0 us)
Async XLA Ops:
  7.2 142.5 %all-gather.2.cloned.1.call-start = ((), (), s32[]{:S(2)}) async-start(), calls=%async_computation.1 | async-start | bytes 8912896 | tf_op jit(solution)/shard_map/all_gather | solution.py:50
  9.3 363.6 %reduce-scatter.2.cloned.1.call-start = ((), (), s32[]{:S(2)}) async-start(), calls=%async_computation.2 | async-start | bytes 8912896 | tf_op jit(solution)/shard_map/reduce_scatter | solution.py:54
  62.5 87.1 %copy-start.5 = (bf16[256,512]{1,0:T(8,128)(2,1)S(1)}, bf16[256,512]{1,0:T(8,128)(2,1)}, u32[]{:S(2)}) copy-start(bf16[256,512]{1,0:T(8,128)(2,1)} %param.9) | copy-start | bytes 786436
  62.5 310.4 %copy-start = (f32[1,512,512]{2,1,0:T(8,128)S(1)}, f32[1,512,512]{2,1,0:T(8,128)}, u32[]{:S(2)}) copy-start(f32[1,512,512]{2,1,0:T(8,128)} %param.11) | copy-start | bytes 3145732
  62.6 310.4 %copy-start.1 = (f32[512,512]{1,0:T(8,128)S(1)}, f32[512,512]{1,0:T(8,128)}, u32[]{:S(2)}) copy-start(f32[512,512]{1,0:T(8,128)} %param.14) | copy-start | bytes 3145732
  62.6 310.4 %copy-start.3 = (bf16[1,512,512]{2,1,0:T(8,128)(2,1)S(1)}, bf16[1,512,512]{2,1,0:T(8,128)(2,1)}, u32[]{:S(2)}) copy-start(bf16[1,512,512]{2,1,0:T(8,128)(2,1)} %param.13) | copy-start | bytes 1572868
  62.6 310.4 %copy-start.4 = (bf16[1,512,512]{2,1,0:T(8,128)(2,1)S(1)}, bf16[1,512,512]{2,1,0:T(8,128)(2,1)}, u32[]{:S(2)}) copy-start(bf16[1,512,512]{2,1,0:T(8,128)(2,1)} %param.12) | copy-start | bytes 1572868
  62.6 439.5 %all-reduce.2.cloned.1.call-start = ((), (), s32[]{:S(2)}) async-start(), calls=%async_computation.3 | async-start | bytes 1048576 | tf_op jit(solution)/shard_map/psum | solution.py:70
  376.2 125.9 %copy-start.2 = (f32[512,512]{1,0:T(8,128)S(1)}, f32[512,512]{1,0:T(8,128)}, u32[]{:S(2)}) copy-start(f32[512,512]{1,0:T(8,128)} %param.15) | copy-start | bytes 3145732
Sparse Core Ops, SparseCore 0:
  11.1 138.4 all-gather.1
  153.7 219.1 reduce-scatter.1
  376.3 125.7 all-reduce.1
where the time goes:
time: 512 us; the launch traced here: 511 us
  waiting for transfers between devices  417 us (81%)
  blocking collectives  39.4 us (8%)
  matrix products  21.2 us (4%)
  other arithmetic  20 us (4%)
  between operations  13.8 us (3%)
    reduce_scatter x1, waiting for transfers between devices, per_device(): lax.psum_scatter((width_scale * contract_first(normed_low, scaled)).astyp...  211 us
    psum x1, waiting for transfers between devices, per_device(): lax.psum(pseudo_grad.astype(jnp.bfloat16), 'replica').astype(jnp.float32)  119 us
    all_gather x1, waiting for transfers between devices, per_device(): lax.all_gather(weight_low, 'fsdp', axis=0, tiled=True)  87 us
    psum x1, blocking collectives, per_device(): answers = lax.psum(jnp.sum(answer), 'fsdp')  39.4 us
    dot_general x1, matrix products, contract_last(): lax.dot_general(left, right, (((1,), (1,)), ((), ())), preferred_element_...  12.5 us
  transfers between devices with their start and end apart: 3, of which 3 were waited for; matrix products, arithmetic and copies ran while one was open for 6% of the time, Pallas kernels for 0%

commit v1 on v0

--- a/solution.py
+++ b/solution.py
@@ -67,7 +67,12 @@
     )
     pseudo_grad = anchor_weight - stepped
     replicas = lax.axis_size("replica")
-    average = lax.psum(pseudo_grad.astype(jnp.bfloat16), "replica").astype(jnp.float32) / replicas
+    average = (
+        jnp.sum(lax.all_gather(pseudo_grad.astype(jnp.bfloat16), "replica"), axis=0).astype(
+            jnp.float32
+        )
+        / replicas
+    )
     new_state = outer_momentum * outer_state + average
     new_anchor = anchor_weight - outer_rate * (average + outer_momentum * new_state)
     new_first = first.astype(jnp.bfloat16)[None]

time: 512 us -> 492 us (0.961)
  waiting for transfers between devices: 417 us -> 402 us
    psum x1 -> x0, waiting for transfers between devices: 119 us -> none  [per_device(): lax.psum(pseudo_grad.astype(jnp.bfloat16), 'replica').astype(jnp.float32)]
    all_gather x1, waiting for transfers between devices: 87 us -> 136 us  [per_device(): lax.all_gather(weight_low, 'fsdp', axis=0, tiled=True)]
    all_gather x0 -> x1, waiting for transfers between devices: none -> 43.7 us  [per_device(): lax.all_gather(pseudo_grad.astype(jnp.bfloat16), 'replica')]
    reduce_scatter x1, waiting for transfers between devices: 211 us -> 222 us  [per_device(): lax.psum_scatter((width_scale * contract_first(normed_low, scaled)).astyp...]
  transfers between devices with their start and end apart: 3 -> 3, of which waited for: 3 -> 3; matrix products, arithmetic and copies ran while one was open for 6% -> 3% of each run, Pallas kernels for 0% -> 0%
where the time goes in v1:
time: 492 us
  waiting for transfers between devices  402 us (82%)
  blocking collectives  39.3 us (8%)
  other arithmetic  18.7 us (4%)
  matrix products  16.7 us (3%)
  between operations  13.8 us (3%)
    reduce_scatter x1, waiting for transfers between devices, per_device(): lax.psum_scatter((width_scale * contract_first(normed_low, scaled)).astyp...  222 us
    all_gather x1, waiting for transfers between devices, per_device(): lax.all_gather(weight_low, 'fsdp', axis=0, tiled=True)  136 us
    all_gather x1, waiting for transfers between devices, per_device(): lax.all_gather(pseudo_grad.astype(jnp.bfloat16), 'replica')  43.7 us
    psum x1, blocking collectives, per_device(): answers = lax.psum(jnp.sum(answer), 'fsdp')  39.3 us
  transfers between devices with their start and end apart: 3, of which 3 were waited for; matrix products, arithmetic and copies ran while one was open for 3% of the time, Pallas kernels for 0%

profile of v1, /device:TPU:1, one launch (start us, length us, event | category | flops | bytes accessed | tf_op | source)
XLA Modules:
  0.0 492.0 jit_solution(17385374985229932692)
XLA Ops:
  7.2 0.0 reduce-scatter.2.cloned.1.call-start
  7.2 1.3 fusion.20
  8.5 0.7 compare_convert_fusion
  9.2 39.3 %psum.7 = f32[]{:T(128)} all-reduce(f32[]{:T(128)} %fusion.20), channel_id=1, replica_groups=mesh['replica'=16,'fsdp'=16] {'fsdp'}, use_global_device_ids=true, to_apply=%region_2.0 | all-reduce | flops 1 | bytes 8 | tf_op jit(solution)/shard_map/psum | solution.py:47
  48.5 3.1 fusion.7
  51.6 8.6 %multiply_convert_fusion = bf16[8192,512]{1,0:T(8,128)(2,1)} fusion(bf16[256,8192]{1,0:T(8,128)(2,1)} %param.8, f32[256]{0:T(256)S(1)} %add_rsqrt_fusion, bf16[256,512]{1,0:T(8,128)(2,1)} %param.9, f32[]{:T(128)} %psum.7, f32[256]{0:T(256)S(1)} %compare_convert_fusion), kind=kOutput, calls=%fused_computation | convolution fusion | flops 2162688000 | bytes 12847108 | tf_op jit(solution)/shard_map/dot_general | solution.py:24
  60.2 0.0 copy-start.1
  60.2 0.0 copy-start.2
  60.2 0.0 copy-start.4
  60.2 0.0 copy-start.5
  60.2 0.0 copy-start.6
  60.2 0.0 reduce-scatter.2.cloned.1.call-update
  60.3 0.0 all-gather.4.cloned.1.call-start
  60.3 1.1 copy-done.1
  61.4 0.9 bitcast_convert_fusion
  62.3 0.0 all-gather.4.cloned.1.call-update
  62.3 0.0 all-gather.6.cloned.1.call-start
  62.4 222.1 %reduce-scatter.2.cloned.1.call-done = bf16[512,512]{1,0:T(8,128)(2,1)} async-done(((bf16[8192,512]{1,0:T(8,128)(2,1)}), bf16[512,512]{1,0:T(8,128)(2,1)}) %reduce-scatter.2.cloned.1.call-update) | async-done | bytes 524304 | tf_op jit(solution)/shard_map/reduce_scatter | solution.py:54
  284.4 0.0 copy-done.2
  284.4 0.0 copy-done.4
  284.4 0.0 copy-done.5
  284.4 3.2 fusion.18
  287.6 0.0 all-gather.6.cloned.1.call-update
  287.6 136.4 %all-gather.4.cloned.1.call-done = bf16[8192,512]{1,0:T(8,128)(2,1)} async-done(((bf16[512,512]{1,0:T(8,128)(2,1)}), bf16[8192,512]{1,0:T(8,128)(2,1)}) %all-gather.4.cloned.1.call-update) | async-done | bytes 8388624 | tf_op jit(solution)/shard_map/all_gather | solution.py:50
  424.1 0.0 copy-done.6
  424.1 0.0 copy-start
  424.1 8.1 %fusion.3 = (f32[256]{0:T(256)S(1)}, f32[256,8192]{1,0:T(8,128)S(1)}) fusion(bf16[256,8192]{1,0:T(8,128)(2,1)} %param.8, f32[256]{0:T(256)S(1)} %add_rsqrt_fusion, bf16[8192,512]{1,0:T(8,128)(2,1)} %all-gather.4.cloned.1.call-done, bf16[256,512]{1,0:T(8,128)(2,1)S(1)} %copy-done.6, f32[]{:T(128)} %psum.7, f32[256]{0:T(256)S(1)} %compare_convert_fusion), kind=kOutput, calls=%fused_computation.7 | convolution fusion | flops 2158493440 | bytes 21236740 | tf_op jit(solution)/shard_map/dot_general | solution.py:18
  432.1 0.0 copy-done
  432.2 3.1 fusion.6
  435.3 0.0 copy-start.3
  435.3 43.7 %all-gather.6.cloned.1.call-done = bf16[8192,512]{1,0:T(8,128)(2,1)} async-done(((bf16[512,512]{1,0:T(8,128)(2,1)}), bf16[8192,512]{1,0:T(8,128)(2,1)}) %all-gather.6.cloned.1.call-update) | async-done | bytes 8388624 | tf_op jit(solution)/shard_map/all_gather | solution.py:71
  479.0 4.8 reduce_sum.42
  483.8 0.0 copy-done.3
  483.8 1.6 multiply_subtract_fusion
  (2 shorter events, 0.0 us)
Async XLA Ops:
  7.2 277.3 %reduce-scatter.2.cloned.1.call-start = ((), (), s32[]{:S(2)}) async-start(), calls=%async_computation.2 | async-start | bytes 8912896 | tf_op jit(solution)/shard_map/reduce_scatter | solution.py:54
  60.2 1.2 copy-start.1
  60.2 224.2 %copy-start.2 = (f32[512,512]{1,0:T(8,128)S(1)}, f32[512,512]{1,0:T(8,128)}, u32[]{:S(2)}) copy-start(f32[512,512]{1,0:T(8,128)} %param.14) | copy-start | bytes 3145732
  60.2 224.2 %copy-start.4 = (bf16[1,512,512]{2,1,0:T(8,128)(2,1)S(1)}, bf16[1,512,512]{2,1,0:T(8,128)(2,1)}, u32[]{:S(2)}) copy-start(bf16[1,512,512]{2,1,0:T(8,128)(2,1)} %param.13) | copy-start | bytes 1572868
  60.2 224.2 %copy-start.5 = (bf16[1,512,512]{2,1,0:T(8,128)(2,1)S(1)}, bf16[1,512,512]{2,1,0:T(8,128)(2,1)}, u32[]{:S(2)}) copy-start(bf16[1,512,512]{2,1,0:T(8,128)(2,1)} %param.12) | copy-start | bytes 1572868
  60.2 363.8 %copy-start.6 = (bf16[256,512]{1,0:T(8,128)(2,1)S(1)}, bf16[256,512]{1,0:T(8,128)(2,1)}, u32[]{:S(2)}) copy-start(bf16[256,512]{1,0:T(8,128)(2,1)} %param.9) | copy-start | bytes 786436
  60.3 363.8 %all-gather.4.cloned.1.call-start = ((), (), s32[]{:S(2)}) async-start(), calls=%async_computation.1 | async-start | bytes 8912896 | tf_op jit(solution)/shard_map/all_gather | solution.py:50
  62.3 416.7 %all-gather.6.cloned.1.call-start = ((), (), s32[]{:S(2)}) async-start(), calls=%async_computation.3 | async-start | bytes 8912896 | tf_op jit(solution)/shard_map/all_gather | solution.py:71
  424.1 8.1 %copy-start = (bf16[256,8192]{1,0:T(8,128)(2,1)S(1)}, bf16[256,8192]{1,0:T(8,128)(2,1)}, u32[]{:S(2)}) copy-start(bf16[256,8192]{1,0:T(8,128)(2,1)} %param.8) | copy-start | bytes 12582916
  435.3 48.5 %copy-start.3 = (f32[512,512]{1,0:T(8,128)S(1)}, f32[512,512]{1,0:T(8,128)}, u32[]{:S(2)}) copy-start(f32[512,512]{1,0:T(8,128)} %param.15) | copy-start | bytes 3145732
Sparse Core Ops, SparseCore 0:
  60.4 223.9 reduce-scatter.1
  287.6 136.4 all-gather.3
  426.5 52.4 all-gather.5

commit v2 on v0

--- a/solution.py
+++ b/solution.py
@@ -47,7 +47,10 @@
     answers = lax.psum(jnp.sum(answer), "fsdp")
     scaled = (cotangent.astype(jnp.float32) * answer[:, None] / answers).astype(jnp.bfloat16)
     feature_grad = width_scale * contract_last(
-        scaled, lax.all_gather(weight_low, "fsdp", axis=0, tiled=True)
+        scaled,
+        jnp.concatenate(
+            lax.all_to_all(jnp.stack([weight_low] * lax.axis_size("fsdp")), "fsdp", 0, 0), axis=0
+        ),
     )
     projected = jnp.mean(feature_grad * normed, axis=1, keepdims=True)
     input_grad = (inverse * (feature_grad - normed * projected)).astype(jnp.bfloat16)

time: 512 us -> 616 us (1.20)
  blocking collectives: 39.4 us -> 213 us
  waiting for transfers between devices: 417 us -> 333 us
  starting transfers between devices: 0.12 us -> 12 us
    psum x1, blocking collectives: 39.4 us -> 213 us  [per_device(): answers = lax.psum(jnp.sum(answer), 'fsdp')]
    all_gather x1 -> x0, waiting for transfers between devices: 87 us -> none  [per_device(): lax.all_gather(weight_low, 'fsdp', axis=0, tiled=True)]
    all_to_all x0 -> x1, starting transfers between devices: none -> 11.9 us  [per_device(): lax.all_to_all(jnp.stack([weight_low] * lax.axis_size('fsdp')), 'fsdp', 0...]
  transfers between devices with their start and end apart: 3 -> 3, of which waited for: 3 -> 2; matrix products, arithmetic and copies ran while one was open for 6% -> 5% of each run, Pallas kernels for 0% -> 0%
where the time goes in v2:
time: 616 us
  waiting for transfers between devices  333 us (54%)
  blocking collectives  213 us (35%)
  matrix products  21.3 us (3%)
  other arithmetic  17.8 us (3%)
  between operations  14.1 us (2%)
  starting transfers between devices  12 us (2%)
    reduce_scatter x1, waiting for transfers between devices, per_device(): lax.psum_scatter((width_scale * contract_first(normed_low, scaled)).astyp...  214 us
    psum x1, blocking collectives, per_device(): answers = lax.psum(jnp.sum(answer), 'fsdp')  213 us
    psum x1, waiting for transfers between devices, per_device(): lax.psum(pseudo_grad.astype(jnp.bfloat16), 'replica').astype(jnp.float32)  119 us
    dot_general x1, matrix products, contract_last(): lax.dot_general(left, right, (((1,), (1,)), ((), ())), preferred_element_...  12.8 us
  transfers between devices with their start and end apart: 3, of which 2 were waited for; matrix products, arithmetic and copies ran while one was open for 5% of the time, Pallas kernels for 0%

profile of v2, /device:TPU:1, one launch (start us, length us, event | category | flops | bytes accessed | tf_op | source)
XLA Modules:
  0.0 615.8 jit_solution(220976325014890108)
XLA Ops:
  7.2 1.3 convert_bitcast_fusion
  8.5 4.0 stack.5
  12.5 0.0 copy-start.5
  12.5 0.0 copy-start.6
  12.5 11.9 %all-to-all-start = ((bf16[16,512,512]{2,1,0:T(8,128)(2,1)}), bf16[16,512,512]{2,1,0:T(8,128)(2,1)}, u32[]{:S(2)}, u32[]{:S(2)}) async-start(bf16[16,512,512]{2,1,0:T(8,128)(2,1)} %stack.5), calls=%async_computation | async-start | bytes 16777216 | tf_op jit(solution)/shard_map/all_to_all | solution.py:52
  24.4 0.0 reduce-scatter.2.cloned.1.call-start
  24.5 0.0 copy-done.5
  24.5 0.6 fusion.20
  25.1 3.1 fusion.7
  28.2 213.1 %psum.14 = f32[]{:T(128)} all-reduce(f32[]{:T(128)} %fusion.20), channel_id=1, replica_groups=mesh['replica'=16,'fsdp'=16] {'fsdp'}, use_global_device_ids=true, to_apply=%region_2.0 | all-reduce | flops 1 | bytes 8 | tf_op jit(solution)/shard_map/psum | solution.py:47
  241.3 0.0 copy-done.6
  241.3 8.6 %multiply_convert_fusion = bf16[8192,512]{1,0:T(8,128)(2,1)} fusion(bf16[256,8192]{1,0:T(8,128)(2,1)} %param.8, f32[256]{0:T(256)S(1)} %add_rsqrt_fusion, bf16[256,512]{1,0:T(8,128)(2,1)S(1)} %copy-done.6, f32[]{:T(128)} %psum.14, f32[256]{0:T(256)S(1)} %compare_convert_fusion), kind=kOutput, calls=%fused_computation | convolution fusion | flops 2162688000 | bytes 12847108 | tf_op jit(solution)/shard_map/dot_general | solution.py:24
  249.9 0.0 reduce-scatter.2.cloned.1.call-update
  249.9 0.0 all-reduce.2.cloned.1.call-start
  249.9 0.0 all-to-all-done
  250.0 0.0 copy-start
  250.0 0.0 copy-start.1
  250.0 0.0 copy-start.3
  250.0 0.0 copy-start.4
  250.0 12.8 %fusion.3 = (f32[256]{0:T(256)S(1)}, f32[256,8192]{1,0:T(8,128)}) fusion(bf16[256,8192]{1,0:T(8,128)(2,1)} %param.8, f32[256]{0:T(256)S(1)} %add_rsqrt_fusion, bf16[8192,512]{1,0:T(8,128)(2,1)} %bitcast.1, bf16[256,512]{1,0:T(8,128)(2,1)S(1)} %copy-done.6, f32[]{:T(128)} %psum.14, f32[256]{0:T(256)S(1)} %compare_convert_fusion), kind=kOutput, calls=%fused_computation.7 | convolution fusion | flops 2158493440 | bytes 21236740 | tf_op jit(solution)/shard_map/dot_general | solution.py:18
  262.8 214.4 %reduce-scatter.2.cloned.1.call-done = bf16[512,512]{1,0:T(8,128)(2,1)} async-done(((bf16[8192,512]{1,0:T(8,128)(2,1)}), bf16[512,512]{1,0:T(8,128)(2,1)}) %reduce-scatter.2.cloned.1.call-update) | async-done | bytes 524304 | tf_op jit(solution)/shard_map/reduce_scatter | solution.py:57
  477.2 0.0 copy-done
  477.2 0.0 copy-done.1
  477.2 0.0 copy-done.3
  477.2 0.0 copy-done.4
  477.2 3.2 fusion.18
  480.4 0.0 all-reduce.2.cloned.1.call-update
  480.4 0.0 copy-start.2
  480.4 6.9 %fusion.6 = bf16[256,8192]{1,0:T(8,128)(2,1)} fusion(f32[256,8192]{1,0:T(8,128)} %get-tuple-element.11, bf16[256,8192]{1,0:T(8,128)(2,1)} %param.8, f32[256]{0:T(256)S(1)} %broadcast_multiply_fusion, f32[256]{0:T(256)S(1)} %add_rsqrt_fusion), kind=kLoop, calls=%fused_computation.10 | loop fusion | flops 12582912 | bytes 16779264 | tf_op jit(solution)/shard_map/convert_element_type | solution.py:56
  487.3 118.9 %all-reduce.2.cloned.1.call-done = bf16[512,512]{1,0:T(8,128)(2,1)} async-done(((bf16[512,512]{1,0:T(8,128)(2,1)}), bf16[512,512]{1,0:T(8,128)(2,1)}) %all-reduce.2.cloned.1.call-update) | async-done | bytes 524304 | tf_op jit(solution)/shard_map/psum | solution.py:73
  606.3 0.0 copy-done.2
  606.3 2.7 multiply_subtract_fusion
  (3 shorter events, 0.0 us)
Async XLA Ops:
  12.5 12.0 %copy-start.5 = (s32[256]{0:T(256)S(1)}, s32[256]{0:T(256)}, u32[]{:S(2)}) copy-start(s32[256]{0:T(256)} %param.10) | copy-start | bytes 3076
  12.5 228.8 %copy-start.6 = (bf16[256,512]{1,0:T(8,128)(2,1)S(1)}, bf16[256,512]{1,0:T(8,128)(2,1)}, u32[]{:S(2)}) copy-start(bf16[256,512]{1,0:T(8,128)(2,1)} %param.9) | copy-start | bytes 786436
  12.5 237.5 %all-to-all-start = ((bf16[16,512,512]{2,1,0:T(8,128)(2,1)}), bf16[16,512,512]{2,1,0:T(8,128)(2,1)}, u32[]{:S(2)}, u32[]{:S(2)}) async-start(bf16[16,512,512]{2,1,0:T(8,128)(2,1)} %stack.5), calls=%async_computation | async-start | bytes 16777216 | tf_op jit(solution)/shard_map/all_to_all | solution.py:52
  24.4 452.8 %reduce-scatter.2.cloned.1.call-start = ((), (), s32[]{:S(2)}) async-start(), calls=%async_computation.2 | async-start | bytes 8912896 | tf_op jit(solution)/shard_map/reduce_scatter | solution.py:57
  249.9 356.4 %all-reduce.2.cloned.1.call-start = ((), (), s32[]{:S(2)}) async-start(), calls=%async_computation.3 | async-start | bytes 1048576 | tf_op jit(solution)/shard_map/psum | solution.py:73
  250.0 227.2 %copy-start = (f32[1,512,512]{2,1,0:T(8,128)S(1)}, f32[1,512,512]{2,1,0:T(8,128)}, u32[]{:S(2)}) copy-start(f32[1,512,512]{2,1,0:T(8,128)} %param.11) | copy-start | bytes 3145732
  250.0 227.2 %copy-start.1 = (f32[512,512]{1,0:T(8,128)S(1)}, f32[512,512]{1,0:T(8,128)}, u32[]{:S(2)}) copy-start(f32[512,512]{1,0:T(8,128)} %param.14) | copy-start | bytes 3145732
  250.0 227.2 %copy-start.3 = (bf16[1,512,512]{2,1,0:T(8,128)(2,1)S(1)}, bf16[1,512,512]{2,1,0:T(8,128)(2,1)}, u32[]{:S(2)}) copy-start(bf16[1,512,512]{2,1,0:T(8,128)(2,1)} %param.13) | copy-start | bytes 1572868
  250.0 227.2 %copy-start.4 = (bf16[1,512,512]{2,1,0:T(8,128)(2,1)S(1)}, bf16[1,512,512]{2,1,0:T(8,128)(2,1)}, u32[]{:S(2)}) copy-start(bf16[1,512,512]{2,1,0:T(8,128)(2,1)} %param.12) | copy-start | bytes 1572868
  480.4 125.9 %copy-start.2 = (f32[512,512]{1,0:T(8,128)S(1)}, f32[512,512]{1,0:T(8,128)}, u32[]{:S(2)}) copy-start(f32[512,512]{1,0:T(8,128)} %param.15) | copy-start | bytes 3145732
Sparse Core Ops, SparseCore 0:
  250.0 227.1 reduce-scatter.1
  480.5 125.7 all-reduce.1
